TPU v7x, 32 devices: a whole 2x2x4 slice. The times are simulated.
32 devices in a mesh: rep: 2 (over y), ctx: 8 (over z, x), head: 2 (over core).
Axes of the slice: x: 2, y: 2, z: 4, core: 2. Of those that a mesh axis runs over, the one named last changes fastest.
Arguments:
- queries: bfloat16 [1024, 32, 128], P(('rep', 'ctx'), 'head'), parts along dimension 0, may hold values from -6 to 6
- keys: bfloat16 [1024, 4, 128], P(('rep', 'ctx'), 'head'), parts along dimension 0, may hold values from -6 to 6
- values: bfloat16 [1024, 4, 128], P(('rep', 'ctx'), 'head'), parts along dimension 0, may hold values from -6 to 6
Outputs:
- attended: bfloat16 [1024, 32, 128], P(('rep', 'ctx'), 'head'), parts along dimension 0
There are 2 independent parts, one for each index of `rep`. A program takes and returns all parts, laid end to end along the dimension named above; each array names one. Nothing has to cross between parts.
All inputs are finite; a program needn't handle non-finite values.
Results may differ from a plain program's by a relative error of at most 0.0037.
Values may be sent and summed in bfloat16 or wider, within the bound.
No kernel may reach another device: no remote copies, remote signals or barrier semaphores. Data moves between devices by JAX's collectives and lax.ppermute only.
A program may use at most 128 MiB of HBM per device.

v0:
```python
import jax
import jax.numpy as jnp
from jax import lax
from jax.sharding import PartitionSpec as P


def from_partner(x, axis, bit):
    return lax.ppermute(x, axis, [(i, i ^ 1 << bit) for i in range(lax.axis_size(axis))])


def attend_piece(state, rows, position, key_piece, value_piece, scale):
    running_max, running_sum, weighted = state
    scores = (
        jnp.einsum("qhgd,khd->hgqk", rows, key_piece, preferred_element_type=jnp.float32) * scale
    )
    key_position = jnp.arange(key_piece.shape[0], dtype=jnp.int32)
    valid = key_position[None, :] <= position[:, None]
    scores = jnp.where(valid, scores, -1e30)
    new_max = jnp.maximum(running_max, jnp.max(scores, axis=-1))
    weights = jnp.where(valid, jnp.exp(scores - new_max[..., None]), 0.0)
    running_sum = jnp.sum(weights, axis=-1)
    update = jnp.einsum(
        "hgqk,khd->hgqd",
        weights.astype(jnp.bfloat16),
        value_piece,
        preferred_element_type=jnp.float32,
    )
    weighted = update
    return (new_max, running_sum, weighted)


def finish(state, half_rows, query_heads, head_size):
    running_max, running_sum, weighted = state
    result = weighted / running_sum[..., None]
    result = jnp.transpose(result, (2, 0, 1, 3)).reshape(half_rows, query_heads, head_size)
    return result.astype(jnp.bfloat16)


def per_device(queries, keys, values):
    local_rows, query_heads, head_size = queries.shape
    key_heads = keys.shape[1]
    group_size = query_heads // key_heads
    half_rows = local_rows // 2
    scale = head_size ** (-0.5)
    context_size = lax.axis_size("ctx")
    position_index = lax.axis_index("ctx")
    offset = jnp.arange(half_rows, dtype=jnp.int32)
    first_rows = queries[:half_rows]
    first_position = position_index * local_rows + offset
    second_rows = queries[half_rows:]
    bit_count = context_size.bit_length() - 1
    for bit_index in range(bit_count):
        second_rows = from_partner(second_rows, "ctx", bit_index)
    second_position = (context_size - 1 - position_index) * local_rows + half_rows + offset
    halves = (
        (first_rows.reshape(half_rows, key_heads, group_size, head_size), first_position),
        (second_rows.reshape(half_rows, key_heads, group_size, head_size), second_position),
    )
    initial = (
        jnp.full((key_heads, group_size, half_rows), -1e30, jnp.float32),
        jnp.zeros((key_heads, group_size, half_rows), jnp.float32),
        jnp.zeros((key_heads, group_size, half_rows, head_size), jnp.float32),
    )
    carries = (initial, initial)
    start = jnp.int32(0)
    key_piece = lax.all_gather(keys, "ctx", axis=0, tiled=True)
    value_piece = lax.all_gather(values, "ctx", axis=0, tiled=True)
    updated = []
    for which in range(2):
        rows, position = halves[which]
        needed = start <= position[-1]
        updated.append(
            lax.cond(
                needed,
                lambda state: attend_piece(state, rows, position, key_piece, value_piece, scale),
                lambda state: state,
                carries[which],
            )
        )
    carries = (updated[0], updated[1])
    first_out = finish(carries[0], half_rows, query_heads, head_size)
    second_out = finish(carries[1], half_rows, query_heads, head_size)
    for bit_index in range(bit_count):
        second_out = from_partner(second_out, "ctx", bit_index)
    return jnp.concatenate([first_out, second_out], axis=0)


def solution(mesh):
    placed = (
        P(("rep", "ctx"), "head", None),
        P(("rep", "ctx"), "head", None),
        P(("rep", "ctx"), "head", None),
    )
    return jax.shard_map(
        per_device,
        mesh=mesh,
        in_specs=placed,
        out_specs=P(("rep", "ctx"), "head", None),
        check_vma=False,
    )
```

profile of v0, /device:TPU:0, one launch (start us, length us, event | category | flops | bytes accessed | tf_op | source)
XLA Modules:
  0.0 91.4 jit_solution(11736791477938292127)
XLA Ops:
  0.0 0.9 slice-done
  0.9 3.0 %collective-permute-start = (bf16[32,16,128]{2,0,1:T(8,128)(2,1)S(1)}, bf16[32,16,128]{2,0,1:T(8,128)(2,1)S(1)}, u32[]{:S(2)}, u32[]{:S(2)}) collective-permute-start(bf16[32,16,128]{2,0,1:T(8,128)(2,1)S(1)} %copy.14), channel_id=1, source_target_pairs={{0,2},{2,0},{4,6},{6,4},{8,10},{10,8},{12,14},{14,12},{1,3},{3,1},... | collective-permute-start | bytes 393224 | tf_op jit(solution)/shard_map/ppermute | solution.py:8
  4.0 3.5 %collective-permute-done = bf16[32,16,128]{2,0,1:T(8,128)(2,1)S(1)} collective-permute-done((bf16[32,16,128]{2,0,1:T(8,128)(2,1)S(1)}, bf16[32,16,128]{2,0,1:T(8,128)(2,1)S(1)}, u32[]{:S(2)}, u32[]{:S(2)}) %collective-permute-start) | collective-permute-done | bytes 131104 | tf_op jit(solution)/shard_map/ppermute | solution.py:8
  7.5 1.8 %collective-permute-start.1 = (bf16[32,16,128]{2,0,1:T(8,128)(2,1)S(1)}, bf16[32,16,128]{2,0,1:T(8,128)(2,1)S(1)}, u32[]{:S(2)}, u32[]{:S(2)}) collective-permute-start(bf16[32,16,128]{2,0,1:T(8,128)(2,1)S(1)} %collective-permute-done), channel_id=1, source_target_pairs={{0,4},{2,6},{4,0},{6,2},{8,12},{10,14},{12,8},{14,10},{1,5},{3,7},... | collective-permute-start | bytes 393224 | tf_op jit(solution)/shard_map/ppermute | solution.py:8
  9.3 0.0 copy-start.2
  9.3 31.0 %all_gather.6 = bf16[512,2,128]{2,0,1:T(8,128)(2,1)S(1)} all-gather(bf16[64,2,128]{2,0,1:T(8,128)(2,1)S(1)} %copy.4), channel_id=1, replica_groups=mesh['rep'=2,'ctx'=8,'head'=2] {'ctx'}, dimensions={0}, use_global_device_ids=true | all-gather | bytes 294912 | tf_op jit(solution)/shard_map/all_gather | solution.py:66
  40.4 0.6 slice.14
  41.6 31.0 %all_gather.7 = bf16[512,2,128]{2,0,1:T(8,128)(2,1)S(1)} all-gather(bf16[64,2,128]{2,0,1:T(8,128)(2,1)S(1)} %copy.5), channel_id=1, replica_groups=mesh['rep'=2,'ctx'=8,'head'=2] {'ctx'}, dimensions={0}, use_global_device_ids=true | all-gather | bytes 294912 | tf_op jit(solution)/shard_map/all_gather | solution.py:67
  72.6 0.0 collective-permute-done.2
  72.6 1.2 %conditional.3 = (f32[2,8,32]{2,1,0:T(8,128)S(1)}, f32[2,8,32,128]{3,2,1,0:T(8,128)S(1)}) conditional(s32[]{:T(128)} %bitcast.15, () %tuple.23, (s32[32]{0:T(128)S(1)}, bf16[32,16,128]{2,0,1:T(8,128)(2,1)S(1)}, bf16[512,2,128]{2,0,1:T(8,128)(2,1)S(1)}, bf16[512,2,128]{2,0,1:T(8,128)(2,1)S(1)}) %tuple.24), branch_computations={%region_4.5_spmd, %region_5.8_spmd} | conditional | flops 136592896 | bytes 4141200 | solution.py:73
  72.6 0.1 iota_compare_fusion.1
  72.7 0.4 fusion.27
  73.1 0.4 fusion.16
  73.4 0.3 fusion.15
  73.8 0.0 copy-start
  73.8 0.1 fusion.25
  73.9 0.1 copy.17
  74.0 0.8 collective-permute-start.3
  74.8 4.2 %collective-permute-done.3 = bf16[32,16,128]{2,1,0:T(8,128)(2,1)S(1)} collective-permute-done((bf16[32,16,128]{2,1,0:T(8,128)(2,1)S(1)}, bf16[32,16,128]{2,1,0:T(8,128)(2,1)S(1)}, u32[]{:S(2)}, u32[]{:S(2)}) %collective-permute-start.3) | collective-permute-done | bytes 131104 | tf_op jit(solution)/shard_map/ppermute | solution.py:8
  79.0 0.6 slice.13
  80.3 1.3 %conditional.2 = (f32[2,8,32]{2,1,0:T(8,128)S(1)}, f32[2,8,32,128]{3,2,1,0:T(8,128)S(1)}) conditional(s32[]{:T(128)} %bitcast.12, () %tuple.21, (s32[32]{0:T(128)S(1)}, bf16[64,16,128]{2,1,0:T(8,128)(2,1)S(1)}, bf16[512,2,128]{2,0,1:T(8,128)(2,1)S(1)}, bf16[512,2,128]{2,0,1:T(8,128)(2,1)S(1)}) %tuple.32), branch_computations={%region_0.0_spmd, %region_1.4_spmd} | conditional | flops 136592896 | bytes 4927632 | solution.py:73
  80.3 0.1 iota_compare_fusion
  80.4 0.1 copy.6
  80.5 0.4 fusion.26
  80.9 0.4 fusion.4
  81.2 0.3 fusion.3
  81.6 2.4 %collective-permute-done.4 = bf16[32,16,128]{2,1,0:T(8,128)(2,1)S(1)} collective-permute-done((bf16[32,16,128]{2,1,0:T(8,128)(2,1)S(1)}, bf16[32,16,128]{2,1,0:T(8,128)(2,1)S(1)}, u32[]{:S(2)}, u32[]{:S(2)}) %collective-permute-start.4) | collective-permute-done | bytes 131104 | tf_op jit(solution)/shard_map/ppermute | solution.py:8
  84.0 0.7 collective-permute-start.5
  84.7 0.1 fusion.24
  84.8 0.1 copy.18
  84.9 5.8 %collective-permute-done.5 = bf16[32,16,128]{2,1,0:T(8,128)(2,1)S(1)} collective-permute-done((bf16[32,16,128]{2,1,0:T(8,128)(2,1)S(1)}, bf16[32,16,128]{2,1,0:T(8,128)(2,1)S(1)}, u32[]{:S(2)}, u32[]{:S(2)}) %collective-permute-start.5) | collective-permute-done | bytes 131104 | tf_op jit(solution)/shard_map/ppermute | solution.py:8
  90.7 0.7 pad_maximum_fusion
  (16 shorter events, 0.1 us)
Async XLA Ops:
  0.0 0.9 slice-start
  0.9 8.4 %copy-start.1 = (bf16[64,2,128]{2,1,0:T(2,128)(2,1)S(1)}, bf16[64,2,128]{2,1,0:T(2,128)(2,1)}, u32[]{:S(2)}) copy-start(bf16[64,2,128]{2,1,0:T(2,128)(2,1)} %param.8) | copy-start | bytes 98308
  0.9 6.5 %collective-permute-start = (bf16[32,16,128]{2,0,1:T(8,128)(2,1)S(1)}, bf16[32,16,128]{2,0,1:T(8,128)(2,1)S(1)}, u32[]{:S(2)}, u32[]{:S(2)}) collective-permute-start(bf16[32,16,128]{2,0,1:T(8,128)(2,1)S(1)} %copy.14), channel_id=1, source_target_pairs={{0,2},{2,0},{4,6},{6,4},{8,10},{10,8},{12,14},{14,12},{1,3},{3,1},... | collective-permute-start | bytes 393224 | tf_op jit(solution)/shard_map/ppermute | solution.py:8
  7.5 32.9 %collective-permute-start.1 = (bf16[32,16,128]{2,0,1:T(8,128)(2,1)S(1)}, bf16[32,16,128]{2,0,1:T(8,128)(2,1)S(1)}, u32[]{:S(2)}, u32[]{:S(2)}) collective-permute-start(bf16[32,16,128]{2,0,1:T(8,128)(2,1)S(1)} %collective-permute-done), channel_id=1, source_target_pairs={{0,4},{2,6},{4,0},{6,2},{8,12},{10,14},{12,8},{14,10},{1,5},{3,7},... | collective-permute-start | bytes 393224 | tf_op jit(solution)/shard_map/ppermute | solution.py:8
  9.3 31.0 %copy-start.2 = (bf16[64,2,128]{2,1,0:T(2,128)(2,1)S(1)}, bf16[64,2,128]{2,1,0:T(2,128)(2,1)}, u32[]{:S(2)}) copy-start(bf16[64,2,128]{2,1,0:T(2,128)(2,1)} %param.9) | copy-start | bytes 98308
  40.4 32.2 %collective-permute-start.2 = (bf16[32,16,128]{2,0,1:T(8,128)(2,1)S(1)}, bf16[32,16,128]{2,0,1:T(8,128)(2,1)S(1)}, u32[]{:S(2)}, u32[]{:S(2)}) collective-permute-start(bf16[32,16,128]{2,0,1:T(8,128)(2,1)S(1)} %collective-permute-done.1), channel_id=1, source_target_pairs={{0,8},{2,10},{4,12},{6,14},{8,0},{10,2},{12,4},{14,6},{1,9},{3,11}... | collective-permute-start | bytes 393224 | tf_op jit(solution)/shard_map/ppermute | solution.py:8
  73.8 6.5 %copy-start = (bf16[64,16,128]{2,1,0:T(8,128)(2,1)S(1)}, bf16[64,16,128]{2,1,0:T(8,128)(2,1)}, u32[]{:S(2)}) copy-start(bf16[64,16,128]{2,1,0:T(8,128)(2,1)} %param.7) | copy-start | bytes 786436
  74.0 5.0 %collective-permute-start.3 = (bf16[32,16,128]{2,1,0:T(8,128)(2,1)S(1)}, bf16[32,16,128]{2,1,0:T(8,128)(2,1)S(1)}, u32[]{:S(2)}, u32[]{:S(2)}) collective-permute-start(bf16[32,16,128]{2,1,0:T(8,128)(2,1)S(1)} %bitcast.51), channel_id=1, source_target_pairs={{0,2},{2,0},{4,6},{6,4},{8,10},{10,8},{12,14},{14,12},{1,3},{3,1},... | collective-permute-start | bytes 393224 | tf_op jit(solution)/shard_map/ppermute | solution.py:8
  79.0 5.0 %collective-permute-start.4 = (bf16[32,16,128]{2,1,0:T(8,128)(2,1)S(1)}, bf16[32,16,128]{2,1,0:T(8,128)(2,1)S(1)}, u32[]{:S(2)}, u32[]{:S(2)}) collective-permute-start(bf16[32,16,128]{2,1,0:T(8,128)(2,1)S(1)} %collective-permute-done.3), channel_id=1, source_target_pairs={{0,4},{2,6},{4,0},{6,2},{8,12},{10,14},{12,8},{14,10},{1,5},{3,7},... | collective-permute-start | bytes 393224 | tf_op jit(solution)/shard_map/ppermute | solution.py:8
  84.0 6.7 %collective-permute-start.5 = (bf16[32,16,128]{2,1,0:T(8,128)(2,1)S(1)}, bf16[32,16,128]{2,1,0:T(8,128)(2,1)S(1)}, u32[]{:S(2)}, u32[]{:S(2)}) collective-permute-start(bf16[32,16,128]{2,1,0:T(8,128)(2,1)S(1)} %collective-permute-done.4), channel_id=1, source_target_pairs={{0,8},{2,10},{4,12},{6,14},{8,0},{10,2},{12,4},{14,6},{1,9},{3,11}... | collective-permute-start | bytes 393224 | tf_op jit(solution)/shard_map/ppermute | solution.py:8
where the time goes:
time: 91.6 us; the launch traced here: 91.4 us
  blocking collectives  62 us (68%)
  waiting for transfers between devices  15.9 us (17%)
  starting transfers between devices  6.41 us (7%)
  local copies, waits for them, and re-layouts  2.32 us (3%)
  other arithmetic  1.85 us (2%)
  matrix products  1.47 us (2%)
  between operations  1.41 us (2%)
    all_gather x1, blocking collectives, per_device(): key_piece = lax.all_gather(keys, 'ctx', axis=0, tiled=True)  31 us
    all_gather x1, blocking collectives, per_device(): value_piece = lax.all_gather(values, 'ctx', axis=0, tiled=True)  31 us
    ppermute x6, waiting for transfers between devices, from_partner(): lax.ppermute(x, axis, [(i, i ^ 1 << bit) for i in range(lax.axis_size(axi...  15.9 us
    ppermute x6, starting transfers between devices, from_partner(): lax.ppermute(x, axis, [(i, i ^ 1 << bit) for i in range(lax.axis_size(axi...  6.41 us
  transfers between devices with their start and end apart: 6, of which 4 were waited for; matrix products, arithmetic and copies ran while one was open for 3% of the time, Pallas kernels for 0%

commit v1 on v0

--- a/solution.py
+++ b/solution.py
@@ -63,7 +63,20 @@
     )
     carries = (initial, initial)
     start = jnp.int32(0)
-    key_piece = lax.all_gather(keys, "ctx", axis=0, tiled=True)
+    opened, upper, state_next = (lax.axis_size("ctx"), lax.axis_index("ctx"), keys.shape[0])
+    local_now, earlier = (keys, 1)
+    while earlier < opened:
+        local_now = jnp.concatenate(
+            [
+                local_now,
+                lax.ppermute(
+                    local_now, "ctx", [(k, (k - earlier) % opened) for k in range(opened)]
+                ),
+            ],
+            0,
+        )
+        earlier = 2 * earlier
+    key_piece = jnp.roll(local_now, upper * state_next, 0)
     value_piece = lax.all_gather(values, "ctx", axis=0, tiled=True)
     updated = []
     for which in range(2):

time: 91.6 us -> 76.3 us (0.83)
  blocking collectives: 62 us -> 31.1 us
  waiting for transfers between devices: 15.9 us -> 24.4 us
  starting transfers between devices: 6.41 us -> 13.3 us
    all_gather x1 -> x0, blocking collectives: 31 us -> none  [per_device(): key_piece = lax.all_gather(keys, 'ctx', axis=0, tiled=True)]
    ppermute x0 -> x3, starting transfers between devices: none -> 6.49 us  [per_device(): lax.ppermute(local_now, 'ctx', [(k, (k - earlier) % opened) for k in rang...]
    ppermute x0 -> x3, waiting for transfers between devices: none -> 5.91 us  [per_device(): lax.ppermute(local_now, 'ctx', [(k, (k - earlier) % opened) for k in rang...]
    ppermute x6, waiting for transfers between devices: 15.9 us -> 18.5 us  [from_partner(): lax.ppermute(x, axis, [(i, i ^ 1 << bit) for i in range(lax.axis_size(axi...]
  transfers between devices with their start and end apart: 6 -> 9, of which waited for: 4 -> 7; matrix products, arithmetic and copies ran while one was open for 3% -> 4% of each run, Pallas kernels for 0% -> 0%
where the time goes in v1:
time: 76.3 us; the launch traced here: 76.1 us
  blocking collectives  31.1 us (41%)
  waiting for transfers between devices  24.4 us (32%)
  starting transfers between devices  13.3 us (17%)
  local copies, waits for them, and re-layouts  2.46 us (3%)
  other arithmetic  1.87 us (2%)
  between operations  1.49 us (2%)
  matrix products  1.47 us (2%)
    all_gather x1, blocking collectives, per_device(): value_piece = lax.all_gather(values, 'ctx', axis=0, tiled=True)  31.1 us
    ppermute x6, waiting for transfers between devices, from_partner(): lax.ppermute(x, axis, [(i, i ^ 1 << bit) for i in range(lax.axis_size(axi...  18.5 us
    ppermute x6, starting transfers between devices, from_partner(): lax.ppermute(x, axis, [(i, i ^ 1 << bit) for i in range(lax.axis_size(axi...  6.79 us
    ppermute x3, starting transfers between devices, per_device(): lax.ppermute(local_now, 'ctx', [(k, (k - earlier) % opened) for k in rang...  6.49 us
    ppermute x3, waiting for transfers between devices, per_device(): lax.ppermute(local_now, 'ctx', [(k, (k - earlier) % opened) for k in rang...  5.91 us
  transfers between devices with their start and end apart: 9, of which 7 were waited for; matrix products, arithmetic and copies ran while one was open for 4% of the time, Pallas kernels for 0%

profile of v1, /device:TPU:0, one launch (start us, length us, event | category | flops | bytes accessed | tf_op | source)
XLA Modules:
  0.0 76.1 jit_solution(13497617495609813109)
XLA Ops:
  0.0 0.9 %slice-done = bf16[32,16,128]{2,1,0:T(8,128)(2,1)S(1)} async-done(((bf16[64,16,128]{2,1,0:T(8,128)(2,1)}), bf16[32,16,128]{2,1,0:T(8,128)(2,1)S(1)}, s32[]{:S(2)}) %slice-start) | async-done | bytes 131096 | tf_op jit(solution)/shard_map/slice | solution.py:50
  0.9 3.0 %collective-permute-start.3 = (bf16[32,16,128]{2,0,1:T(8,128)(2,1)S(1)}, bf16[32,16,128]{2,0,1:T(8,128)(2,1)S(1)}, u32[]{:S(2)}, u32[]{:S(2)}) collective-permute-start(bf16[32,16,128]{2,0,1:T(8,128)(2,1)S(1)} %copy.18), channel_id=1, source_target_pairs={{0,2},{2,0},{4,6},{6,4},{8,10},{10,8},{12,14},{14,12},{1,3},{3,1},... | collective-permute-start | bytes 393224 | tf_op jit(solution)/shard_map/ppermute | solution.py:8
  4.0 3.7 %collective-permute-start = (bf16[64,2,128]{2,0,1:T(8,128)(2,1)S(1)}, bf16[64,2,128]{2,0,1:T(8,128)(2,1)S(1)}, u32[]{:S(2)}, u32[]{:S(2)}) collective-permute-start(bf16[64,2,128]{2,0,1:T(8,128)(2,1)S(1)} %get-tuple-element.48), channel_id=1, source_target_pairs={{0,14},{2,0},{4,2},{6,4},{8,6},{10,8},{12,10},{14,12},{1,15},{3,1}... | collective-permute-start | bytes 98312 | tf_op jit(solution)/shard_map/ppermute | solution.py:72
  7.8 0.6 slice.14
  9.0 0.3 collective-permute-done
  9.4 2.7 %collective-permute-start.1 = (bf16[128,2,128]{2,0,1:T(8,128)(2,1)S(1)}, bf16[128,2,128]{2,0,1:T(8,128)(2,1)S(1)}, u32[]{:S(2)}, u32[]{:S(2)}) collective-permute-start(bf16[128,2,128]{2,0,1:T(8,128)(2,1)S(1)} %pad_maximum_fusion.2), channel_id=1, source_target_pairs={{0,12},{2,14},{4,0},{6,2},{8,4},{10,6},{12,8},{14,10},{1,13},{3,15... | collective-permute-start | bytes 196616 | tf_op jit(solution)/shard_map/ppermute | solution.py:72
  12.0 31.1 %all_gather.3 = bf16[512,2,128]{2,0,1:T(8,128)(2,1)S(1)} all-gather(bf16[64,2,128]{2,0,1:T(8,128)(2,1)S(1)} %copy.9), channel_id=1, replica_groups=mesh['rep'=2,'ctx'=8,'head'=2] {'ctx'}, dimensions={0}, use_global_device_ids=true | all-gather | bytes 294912 | tf_op jit(solution)/shard_map/all_gather | solution.py:80
  43.1 0.1 collective-permute-start.2
  43.3 1.2 %collective-permute-start.4 = (bf16[32,16,128]{2,0,1:T(8,128)(2,1)S(1)}, bf16[32,16,128]{2,0,1:T(8,128)(2,1)S(1)}, u32[]{:S(2)}, u32[]{:S(2)}) collective-permute-start(bf16[32,16,128]{2,0,1:T(8,128)(2,1)S(1)} %collective-permute-done.3), channel_id=1, source_target_pairs={{0,4},{2,6},{4,0},{6,2},{8,12},{10,14},{12,8},{14,10},{1,5},{3,7},... | collective-permute-start | bytes 393224 | tf_op jit(solution)/shard_map/ppermute | solution.py:8
  44.4 5.6 %collective-permute-done.2 = bf16[256,2,128]{2,0,1:T(8,128)(2,1)S(1)} collective-permute-done((bf16[256,2,128]{2,0,1:T(8,128)(2,1)S(1)}, bf16[256,2,128]{2,0,1:T(8,128)(2,1)S(1)}, u32[]{:S(2)}, u32[]{:S(2)}) %collective-permute-start.2) | collective-permute-done | bytes 131104 | tf_op jit(solution)/shard_map/ppermute | solution.py:72
  50.1 0.9 %collective-permute-done.4 = bf16[32,16,128]{2,0,1:T(8,128)(2,1)S(1)} collective-permute-done((bf16[32,16,128]{2,0,1:T(8,128)(2,1)S(1)}, bf16[32,16,128]{2,0,1:T(8,128)(2,1)S(1)}, u32[]{:S(2)}, u32[]{:S(2)}) %collective-permute-start.4) | collective-permute-done | bytes 131104 | tf_op jit(solution)/shard_map/ppermute | solution.py:8
  51.0 0.2 collective-permute-start.5
  51.2 6.0 %collective-permute-done.5 = bf16[32,16,128]{2,0,1:T(8,128)(2,1)S(1)} collective-permute-done((bf16[32,16,128]{2,0,1:T(8,128)(2,1)S(1)}, bf16[32,16,128]{2,0,1:T(8,128)(2,1)S(1)}, u32[]{:S(2)}, u32[]{:S(2)}) %collective-permute-start.5) | collective-permute-done | bytes 131104 | tf_op jit(solution)/shard_map/ppermute | solution.py:8
  57.2 1.2 %conditional.3 = (f32[2,8,32]{2,1,0:T(8,128)S(1)}, f32[2,8,32,128]{3,2,1,0:T(8,128)S(1)}) conditional(s32[]{:T(128)} %bitcast.15, () %tuple.23, (s32[32]{0:T(128)S(1)}, bf16[32,16,128]{2,0,1:T(8,128)(2,1)S(1)}, bf16[512,2,128]{2,0,1:T(8,128)(2,1)S(1)}, bf16[512,2,128]{2,0,1:T(8,128)(2,1)S(1)}) %tuple.24), branch_computations={%region_4.5_spmd, %region_5.8_spmd} | conditional | flops 136592896 | bytes 4141200 | solution.py:86
  57.2 0.1 iota_compare_fusion.1
  57.3 0.4 fusion.27
  57.7 0.3 fusion.15
  58.1 0.4 fusion.16
  58.4 0.1 fusion.25
  58.6 1.8 %collective-permute-start.6 = (bf16[32,16,128]{2,1,0:T(8,128)(2,1)S(1)}, bf16[32,16,128]{2,1,0:T(8,128)(2,1)S(1)}, u32[]{:S(2)}, u32[]{:S(2)}) collective-permute-start(bf16[32,16,128]{2,1,0:T(8,128)(2,1)S(1)} %bitcast.51), channel_id=1, source_target_pairs={{0,2},{2,0},{4,6},{6,4},{8,10},{10,8},{12,14},{14,12},{1,3},{3,1},... | collective-permute-start | bytes 393224 | tf_op jit(solution)/shard_map/ppermute | solution.py:8
  60.4 3.3 %collective-permute-done.6 = bf16[32,16,128]{2,1,0:T(8,128)(2,1)S(1)} collective-permute-done((bf16[32,16,128]{2,1,0:T(8,128)(2,1)S(1)}, bf16[32,16,128]{2,1,0:T(8,128)(2,1)S(1)}, u32[]{:S(2)}, u32[]{:S(2)}) %collective-permute-start.6) | collective-permute-done | bytes 131104 | tf_op jit(solution)/shard_map/ppermute | solution.py:8
  63.7 0.6 slice.13
  64.9 1.3 %conditional.2 = (f32[2,8,32]{2,1,0:T(8,128)S(1)}, f32[2,8,32,128]{3,2,1,0:T(8,128)S(1)}) conditional(s32[]{:T(128)} %bitcast.12, () %tuple.21, (s32[32]{0:T(128)S(1)}, bf16[64,16,128]{2,1,0:T(8,128)(2,1)S(1)}, bf16[512,2,128]{2,0,1:T(8,128)(2,1)S(1)}, bf16[512,2,128]{2,0,1:T(8,128)(2,1)S(1)}) %tuple.33), branch_computations={%region_0.1_spmd, %region_1.4_spmd} | conditional | flops 136592896 | bytes 4927632 | solution.py:86
  65.1 0.1 iota_compare_fusion
  65.1 0.4 fusion.26
  65.5 0.3 fusion.3
  65.9 0.4 fusion.4
  66.2 2.4 %collective-permute-done.7 = bf16[32,16,128]{2,1,0:T(8,128)(2,1)S(1)} collective-permute-done((bf16[32,16,128]{2,1,0:T(8,128)(2,1)S(1)}, bf16[32,16,128]{2,1,0:T(8,128)(2,1)S(1)}, u32[]{:S(2)}, u32[]{:S(2)}) %collective-permute-start.7) | collective-permute-done | bytes 131104 | tf_op jit(solution)/shard_map/ppermute | solution.py:8
  68.7 0.6 collective-permute-start.8
  69.3 0.1 fusion.24
  69.5 5.9 %collective-permute-done.8 = bf16[32,16,128]{2,1,0:T(8,128)(2,1)S(1)} collective-permute-done((bf16[32,16,128]{2,1,0:T(8,128)(2,1)S(1)}, bf16[32,16,128]{2,1,0:T(8,128)(2,1)S(1)}, u32[]{:S(2)}, u32[]{:S(2)}) %collective-permute-start.8) | collective-permute-done | bytes 131104 | tf_op jit(solution)/shard_map/ppermute | solution.py:8
  75.4 0.7 pad_maximum_fusion
  (31 shorter events, 0.4 us)
Async XLA Ops:
  0.0 0.9 %slice-start = ((bf16[64,16,128]{2,1,0:T(8,128)(2,1)}), bf16[32,16,128]{2,1,0:T(8,128)(2,1)S(1)}, s32[]{:S(2)}) async-start(bf16[64,16,128]{2,1,0:T(8,128)(2,1)} %param.7), calls=%async_computation | async-start | bytes 262144 | tf_op jit(solution)/shard_map/slice | solution.py:50
  0.9 3.1 %copy-start.1 = (bf16[64,2,128]{2,1,0:T(2,128)(2,1)S(1)}, bf16[64,2,128]{2,1,0:T(2,128)(2,1)}, u32[]{:S(2)}) copy-start(bf16[64,2,128]{2,1,0:T(2,128)(2,1)} %param.8) | copy-start | bytes 98308
  0.9 42.3 %collective-permute-start.3 = (bf16[32,16,128]{2,0,1:T(8,128)(2,1)S(1)}, bf16[32,16,128]{2,0,1:T(8,128)(2,1)S(1)}, u32[]{:S(2)}, u32[]{:S(2)}) collective-permute-start(bf16[32,16,128]{2,0,1:T(8,128)(2,1)S(1)} %copy.18), channel_id=1, source_target_pairs={{0,2},{2,0},{4,6},{6,4},{8,10},{10,8},{12,14},{14,12},{1,3},{3,1},... | collective-permute-start | bytes 393224 | tf_op jit(solution)/shard_map/ppermute | solution.py:8
  4.0 5.0 %copy-start.2 = (bf16[64,2,128]{2,1,0:T(2,128)(2,1)S(1)}, bf16[64,2,128]{2,1,0:T(2,128)(2,1)}, u32[]{:S(2)}) copy-start(bf16[64,2,128]{2,1,0:T(2,128)(2,1)} %param.9) | copy-start | bytes 98308
  4.0 5.3 %collective-permute-start = (bf16[64,2,128]{2,0,1:T(8,128)(2,1)S(1)}, bf16[64,2,128]{2,0,1:T(8,128)(2,1)S(1)}, u32[]{:S(2)}, u32[]{:S(2)}) collective-permute-start(bf16[64,2,128]{2,0,1:T(8,128)(2,1)S(1)} %get-tuple-element.48), channel_id=1, source_target_pairs={{0,14},{2,0},{4,2},{6,4},{8,6},{10,8},{12,10},{14,12},{1,15},{3,1}... | collective-permute-start | bytes 98312 | tf_op jit(solution)/shard_map/ppermute | solution.py:72
  9.4 33.8 %collective-permute-start.1 = (bf16[128,2,128]{2,0,1:T(8,128)(2,1)S(1)}, bf16[128,2,128]{2,0,1:T(8,128)(2,1)S(1)}, u32[]{:S(2)}, u32[]{:S(2)}) collective-permute-start(bf16[128,2,128]{2,0,1:T(8,128)(2,1)S(1)} %pad_maximum_fusion.2), channel_id=1, source_target_pairs={{0,12},{2,14},{4,0},{6,2},{8,4},{10,6},{12,8},{14,10},{1,13},{3,15... | collective-permute-start | bytes 196616 | tf_op jit(solution)/shard_map/ppermute | solution.py:72
  43.1 6.9 %collective-permute-start.2 = (bf16[256,2,128]{2,0,1:T(8,128)(2,1)S(1)}, bf16[256,2,128]{2,0,1:T(8,128)(2,1)S(1)}, u32[]{:S(2)}, u32[]{:S(2)}) collective-permute-start(bf16[256,2,128]{2,0,1:T(8,128)(2,1)S(1)} %pad_maximum_fusion.1), channel_id=1, source_target_pairs={{0,8},{2,10},{4,12},{6,14},{8,0},{10,2},{12,4},{14,6},{1,9},{3,11}... | collective-permute-start | bytes 393224 | tf_op jit(solution)/shard_map/ppermute | solution.py:72
  43.3 7.7 %collective-permute-start.4 = (bf16[32,16,128]{2,0,1:T(8,128)(2,1)S(1)}, bf16[32,16,128]{2,0,1:T(8,128)(2,1)S(1)}, u32[]{:S(2)}, u32[]{:S(2)}) collective-permute-start(bf16[32,16,128]{2,0,1:T(8,128)(2,1)S(1)} %collective-permute-done.3), channel_id=1, source_target_pairs={{0,4},{2,6},{4,0},{6,2},{8,12},{10,14},{12,8},{14,10},{1,5},{3,7},... | collective-permute-start | bytes 393224 | tf_op jit(solution)/shard_map/ppermute | solution.py:8
  51.0 6.3 %collective-permute-start.5 = (bf16[32,16,128]{2,0,1:T(8,128)(2,1)S(1)}, bf16[32,16,128]{2,0,1:T(8,128)(2,1)S(1)}, u32[]{:S(2)}, u32[]{:S(2)}) collective-permute-start(bf16[32,16,128]{2,0,1:T(8,128)(2,1)S(1)} %collective-permute-done.4), channel_id=1, source_target_pairs={{0,8},{2,10},{4,12},{6,14},{8,0},{10,2},{12,4},{14,6},{1,9},{3,11}... | collective-permute-start | bytes 393224 | tf_op jit(solution)/shard_map/ppermute | solution.py:8
  58.4 6.5 %copy-start = (bf16[64,16,128]{2,1,0:T(8,128)(2,1)S(1)}, bf16[64,16,128]{2,1,0:T(8,128)(2,1)}, u32[]{:S(2)}) copy-start(bf16[64,16,128]{2,1,0:T(8,128)(2,1)} %param.7) | copy-start | bytes 786436
  58.6 5.0 %collective-permute-start.6 = (bf16[32,16,128]{2,1,0:T(8,128)(2,1)S(1)}, bf16[32,16,128]{2,1,0:T(8,128)(2,1)S(1)}, u32[]{:S(2)}, u32[]{:S(2)}) collective-permute-start(bf16[32,16,128]{2,1,0:T(8,128)(2,1)S(1)} %bitcast.51), channel_id=1, source_target_pairs={{0,2},{2,0},{4,6},{6,4},{8,10},{10,8},{12,14},{14,12},{1,3},{3,1},... | collective-permute-start | bytes 393224 | tf_op jit(solution)/shard_map/ppermute | solution.py:8
  63.7 5.0 %collective-permute-start.7 = (bf16[32,16,128]{2,1,0:T(8,128)(2,1)S(1)}, bf16[32,16,128]{2,1,0:T(8,128)(2,1)S(1)}, u32[]{:S(2)}, u32[]{:S(2)}) collective-permute-start(bf16[32,16,128]{2,1,0:T(8,128)(2,1)S(1)} %collective-permute-done.6), channel_id=1, source_target_pairs={{0,4},{2,6},{4,0},{6,2},{8,12},{10,14},{12,8},{14,10},{1,5},{3,7},... | collective-permute-start | bytes 393224 | tf_op jit(solution)/shard_map/ppermute | solution.py:8
  68.7 6.7 %collective-permute-start.8 = (bf16[32,16,128]{2,1,0:T(8,128)(2,1)S(1)}, bf16[32,16,128]{2,1,0:T(8,128)(2,1)S(1)}, u32[]{:S(2)}, u32[]{:S(2)}) collective-permute-start(bf16[32,16,128]{2,1,0:T(8,128)(2,1)S(1)} %collective-permute-done.7), channel_id=1, source_target_pairs={{0,8},{2,10},{4,12},{6,14},{8,0},{10,2},{12,4},{14,6},{1,9},{3,11}... | collective-permute-start | bytes 393224 | tf_op jit(solution)/shard_map/ppermute | solution.py:8
